TPU v7x, 128 devices: a whole 4x4x4 slice. The times are simulated.
128 devices in a mesh: dp: 4 (over x), seq: 8 (over z, core), expert: 4 (over y).
Axes of the slice: x: 4, y: 4, z: 4, core: 2. Of those that a mesh axis runs over, the one named last changes fastest.
Arguments:
- x_in: bfloat16 [4096, 8192], P(('dp', 'seq'), 'expert'), parts along dimension 0, may hold values from -6 to 6
- z_in: bfloat16 [4096, 8192], P(('dp', 'seq'), 'expert'), parts along dimension 0, may hold values from -6 to 6
- step_raw: bfloat16 [4096, 8192], P(('dp', 'seq'), 'expert'), parts along dimension 0, may hold values from -4 to 4
- step_bias: float32 [8192], P('expert'), may hold values from -9 to -2
- decay_rate: float32 [16, 8192], P(None, 'expert'), may hold values from 0.5 to 4
- b_coef: bfloat16 [16, 4096], P(None, ('dp', 'seq')), parts along dimension 1, may hold values from -6 to 6
- c_coef: bfloat16 [16, 4096], P(None, ('dp', 'seq')), parts along dimension 1, may hold values from -6 to 6
- skip_gain: float32 [8192], P('expert'), may hold values from 0.5 to 1.5
- out_proj: bfloat16 [8192, 8192], P('expert', 'seq'), may hold values from -0.0625 to 0.0625
- residual: bfloat16 [4096, 8192], P(('dp', 'seq', 'expert')), parts along dimension 0, may hold values from -6 to 6
- norm_gain: float32 [8192], replicated, may hold values from 0.5 to 1.5
- router_weight: bfloat16 [8192, 16], replicated, may hold values from -0.0625 to 0.0625
- expert_ids: int32 [4096, 2], P(('dp', 'seq', 'expert')), parts along dimension 0, may hold values from 0 to 15, as said below
- gate_weight: bfloat16 [8192, 12288], P(None, ('seq', 'expert')), may hold values from -0.0625 to 0.0625
- up_weight: bfloat16 [8192, 12288], P(None, ('seq', 'expert')), may hold values from -0.0625 to 0.0625
- down_weight: bfloat16 [12288, 8192], P(('seq', 'expert')), may hold values from -0.0546875 to 0.0546875
Outputs:
- final: bfloat16 [4096, 8192], P(('dp', 'seq', 'expert')), parts along dimension 0
There are 4 independent parts, one for each index of `dp`. A program takes and returns all parts, laid end to end along the dimension named above; an argument that names none is the same for every part. Nothing has to cross between parts.
Inputs may be any that keep to these rules, and one draw needn't show every extreme that they name: `expert_ids`: each token names 2 different experts; among the 32 rows of one device at most 16 name expert 0 and at least one does; on some device exactly 16 do.
All inputs are finite; a program needn't handle non-finite values.
Results may differ from a plain program's by a relative error of at most 0.006.
Values may be sent and summed in bfloat16 or wider, within the bound.
No kernel may reach another device: no remote copies, remote signals or barrier semaphores. Data moves between devices by JAX's collectives and lax.ppermute only.
A program may use at most 192 MiB of HBM per device.

v0:
```python
import jax
import jax.numpy as jnp
from jax import lax
from jax.sharding import PartitionSpec as P

BLOCK = 128


def entering(value, axis, join, neutral):
    count, mine = (lax.axis_size(axis), lax.axis_index(axis))
    pieces = jax.tree.map(lambda part: lax.all_gather(part, axis), value)
    running = jax.tree.map(
        lambda part, zero: jnp.full_like(part, 0) + jnp.asarray(zero, part.dtype), value, neutral
    )

    def hop(position, running):
        longer = join(running, jax.tree.map(lambda part: part[position], pieces))
        return jax.tree.map(lambda new, old: jnp.where(position < mine, new, old), longer, running)

    return lax.fori_loop(0, count - 1, hop, running)


def pair_combine(early, later):
    return (early[0] * later[0], later[0] * early[1] + later[1])


def end_state(step_size, x_float, decay_rate, b_rows):

    def end_advance(state, inputs):
        step_now, x_now, b_now = inputs
        state = (
            jnp.exp(-step_now[None, :] * decay_rate) * state
            + (step_now * x_now)[None, :] * b_now[:, None]
        )
        return (state, None)

    start_state = jnp.zeros(decay_rate.shape, jnp.float32)
    final_state, _ = lax.scan(end_advance, start_state, (step_size, x_float, b_rows), unroll=8)
    return final_state


def scan_outputs(state_in, step_size, x_float, decay_rate, b_rows, c_rows, skip_gain):

    def scan_advance(state, inputs):
        step_now, x_now, b_now, c_now = inputs
        state = (
            jnp.exp(-step_now[None, :] * decay_rate) * state
            + (step_now * x_now)[None, :] * b_now[:, None]
        )
        y_now = jnp.sum(c_now[:, None] * state, axis=0) + skip_gain * x_now
        return (state, y_now)

    _, outputs = lax.scan(scan_advance, state_in, (step_size, x_float, b_rows, c_rows), unroll=8)
    return outputs


def on_device(
    x_in,
    z_in,
    step_raw,
    step_bias,
    decay_rate,
    b_coef,
    c_coef,
    skip_gain,
    out_proj,
    residual,
    norm_gain,
    router_weight,
    expert_ids,
    gate_weight,
    up_weight,
    down_weight,
):
    step_size = jax.nn.softplus(step_raw.astype(jnp.float32) + step_bias[None, :])
    x_float = x_in.astype(jnp.float32)
    b_rows = b_coef.astype(jnp.float32).T
    c_rows = c_coef.astype(jnp.float32).T
    state_end = end_state(step_size, x_float, decay_rate, b_rows)
    decay_end = jnp.exp(-decay_rate * jnp.sum(step_size, axis=0)[None, :])
    identity = (jnp.ones_like(decay_end), jnp.zeros_like(state_end))
    carried = entering((decay_end, state_end), "seq", pair_combine, identity)
    state_in = carried[1]
    scanned = scan_outputs(state_in, step_size, x_float, decay_rate, b_rows, c_rows, skip_gain)
    gated = (scanned * jax.nn.silu(z_in.astype(jnp.float32))).astype(jnp.bfloat16)
    column_part = jnp.dot(
        lax.all_gather(gated, "seq", axis=0, tiled=True),
        out_proj,
        preferred_element_type=jnp.float32,
    )
    seq_count = lax.axis_size("seq")
    expert_count = lax.axis_size("expert")
    rows = residual.shape[0]
    grouped = column_part.reshape(seq_count, expert_count, rows, column_part.shape[1])
    summed = lax.psum_scatter(grouped, "expert", scatter_dimension=1, tiled=True)
    arranged = jnp.transpose(summed[:, 0], (1, 0, 2))
    swapped = lax.all_to_all(arranged, "seq", split_axis=1, concat_axis=1, tiled=True)
    mamba_out = swapped.reshape(rows, -1)
    hidden = (residual.astype(jnp.float32) + mamba_out).astype(jnp.bfloat16)
    hidden_f = hidden.astype(jnp.float32)
    width_d = hidden.shape[1]
    scale_cols = width_d // BLOCK
    normed = (
        hidden_f
        * lax.rsqrt(jnp.mean(hidden_f * hidden_f, axis=-1, keepdims=True) + 1e-05)
        * norm_gain[None, :]
    )
    blocked = normed.reshape(rows, scale_cols, BLOCK)
    scales = (jnp.max(jnp.abs(blocked), axis=-1) / 448.0 + 1e-06).astype(jnp.bfloat16)
    quant = (blocked / scales.astype(jnp.float32)[..., None]).astype(jnp.bfloat16)
    restored = (
        (quant.astype(jnp.float32) * scales.astype(jnp.float32)[..., None])
        .astype(jnp.bfloat16)
        .reshape(rows, width_d)
    )
    experts = router_weight.shape[1]
    probs = jax.nn.sigmoid(jnp.dot(restored, router_weight, preferred_element_type=jnp.float32))
    picks = expert_ids[:, :, None] == jnp.arange(experts, dtype=jnp.int32)[None, None, :]
    chosen = jnp.sum(jnp.where(picks, probs[:, None, :], jnp.float32(0.0)), axis=-1)
    weights = chosen / jnp.sum(chosen, axis=-1, keepdims=True)
    coef = jnp.sum(jnp.where(expert_ids == 0, weights, jnp.float32(0.0)), axis=1)
    wanted = jnp.any(expert_ids == 0, axis=1)
    wanted_int = wanted.astype(jnp.int32)
    slot_pos = jnp.cumsum(wanted_int) - wanted_int
    capacity = rows // 2
    table = (
        (slot_pos[None, :] == jnp.arange(capacity, dtype=jnp.int32)[:, None]) & wanted[None, :]
    ).astype(jnp.bfloat16)
    send_quant = jnp.dot(
        table, quant.reshape(rows, width_d), preferred_element_type=jnp.float32
    ).astype(jnp.bfloat16)
    send_scale = jnp.dot(table, scales, preferred_element_type=jnp.float32).astype(jnp.bfloat16)
    all_quant, all_scale = (
        lax.all_gather(send_quant, ("seq", "expert"), axis=0, tiled=True),
        lax.all_gather(send_scale, ("seq", "expert"), axis=0, tiled=True),
    )
    slots = all_quant.shape[0]
    inputs = (
        (
            all_quant.reshape(slots, scale_cols, BLOCK).astype(jnp.float32)
            * all_scale.astype(jnp.float32)[..., None]
        )
        .astype(jnp.bfloat16)
        .reshape(slots, width_d)
    )
    gate_value = jnp.dot(inputs, gate_weight, preferred_element_type=jnp.float32)
    up_value = jnp.dot(inputs, up_weight, preferred_element_type=jnp.float32)
    active = (jax.nn.silu(gate_value) * up_value).astype(jnp.bfloat16)
    own_sum = lax.psum_scatter(
        jnp.dot(active, down_weight, preferred_element_type=jnp.float32).astype(jnp.bfloat16),
        ("seq", "expert"),
        scatter_dimension=0,
        tiled=True,
    )
    returned = jnp.dot(table.T, own_sum, preferred_element_type=jnp.float32)
    return (hidden_f + coef[:, None] * returned).astype(jnp.bfloat16)


def solution(mesh):
    return jax.shard_map(
        on_device,
        mesh=mesh,
        in_specs=(
            P(("dp", "seq"), "expert"),
            P(("dp", "seq"), "expert"),
            P(("dp", "seq"), "expert"),
            P("expert"),
            P(None, "expert"),
            P(None, ("dp", "seq")),
            P(None, ("dp", "seq")),
            P("expert"),
            P("expert", "seq"),
            P(("dp", "seq", "expert"), None),
            P(),
            P(),
            P(("dp", "seq", "expert"), None),
            P(None, ("seq", "expert")),
            P(None, ("seq", "expert")),
            P(("seq", "expert"), None),
        ),
        out_specs=P(("dp", "seq", "expert"), None),
        check_vma=False,
    )
```

profile of v0, /device:TPU:0, one launch (start us, length us, event | category | flops | bytes accessed | tf_op | source)
XLA Modules:
  0.0 533.8 jit_solution(4677953557653513335)
XLA Ops:
  8.5 1.7 fusion.67
  10.2 21.8 %while.38 = (s32[]{:T(128)}, f32[16,2048]{1,0:T(8,128)S(1)}, f32[16,8,2048]{2,1,0:T(8,128)S(1)}, f32[16,2048]{1,0:T(8,128)}, f32[16,8,2048]{2,1,0:T(8,128)S(1)},...) while((s32[]{:T(128)}, f32[16,2048]{1,0:T(8,128)S(1)}, ...), condition=%wide.region_2.3_spmd.clone, body=%wide.region_1.2_spmd.clone.sunk | while | flops 1114122 | bytes 789271 | solution.py:38
  32.8 1.6 multiply_exponential_fusion
  34.6 24.2 %all-gather.13.cloned.1.call-done = f32[128,2048]{1,0:T(8,128)} async-done(((f32[16,2048]{1,0:T(8,128)}), f32[128,2048]{1,0:T(8,128)}) %all-gather.13.cloned.1.call-update) | async-done | bytes 1048592 | tf_op jit(solution)/shard_map/all_gather | solution.py:11
  58.8 25.1 %all-gather.11.cloned.1.call-done = f32[128,2048]{1,0:T(8,128)} async-done(((f32[16,2048]{1,0:T(8,128)}), f32[128,2048]{1,0:T(8,128)}) %all-gather.11.cloned.1.call-update) | async-done | bytes 1048592 | tf_op jit(solution)/shard_map/all_gather | solution.py:11
  84.0 7.6 %while.39 = (s32[]{:T(128)}, f32[16,2048]{1,0:T(8,128)S(1)}, s32[]{:T(128)}, f32[8,16,2048]{2,1,0:T(8,128)}, f32[8,16,2048]{2,1,0:T(8,128)}, /*index=5*/s32[]{:T(128)}, s32[]{:T(128)}) while((s32[]{:T(128)}, f32[16,2048]{1,0:T(8,128)S(1)}, s32[]{:T(128)}, f32[8,16,2048]{2,1,0:T(8,128)}, f32[8,16,2048]{2,1,0:T(8,128)}, ...), condition=%wide.region_4.5_spmd.clone, body=%wide.region_3.4_spmd.clone.sunk | while | flops 131076 | bytes 524397 | solution.py:20
  91.6 71.2 %while.37 = (s32[]{:T(128)}, f32[16,2048]{1,0:T(8,128)S(1)}, f32[16,8,2048]{2,1,0:T(8,128)}, f32[16,8,2048]{2,1,0:T(8,128)S(1)}, f32[16,2048]{1,0:T(8,128)}, /*i...) while((s32[]{:T(128)}, f32[16,2048]{1,0:T(8,128)S(1)}, ...), condition=%wide.region_14.15_spmd, body=%wide.region_5.14_spmd.sunk | while | flops 2408457 | bytes 2078409 | solution.py:53
  97.3 1.2 multiply_reduce_fusion.11
  106.2 1.2 multiply_reduce_fusion.11
  110.7 1.2 multiply_reduce_fusion.11
  119.6 1.2 multiply_reduce_fusion.11
  124.0 1.2 multiply_reduce_fusion.11
  128.5 1.2 multiply_reduce_fusion.11
  132.9 1.2 multiply_reduce_fusion.11
  137.4 1.2 multiply_reduce_fusion.11
  141.8 1.2 multiply_reduce_fusion.11
  150.7 1.2 multiply_reduce_fusion.11
  159.6 1.2 multiply_reduce_fusion.11
  162.8 2.3 fusion.66
  165.2 32.3 %all-gather.7.cloned.1.call-done = bf16[1024,2048]{1,0:T(8,128)(2,1)} async-done(((bf16[128,2048]{1,0:T(8,128)(2,1)}), bf16[1024,2048]{1,0:T(8,128)(2,1)}) %all-gather.7.cloned.1.call-update) | async-done | bytes 4194320 | tf_op jit(solution)/shard_map/all_gather | solution.py:87
  197.5 9.9 %fusion.91 = f32[1024,1024]{1,0:T(8,128)} fusion(bf16[1024,2048]{1,0:T(8,128)(2,1)} %all-gather.7.cloned.1.call-done, bf16[2048,1024]{1,0:T(8,128)(2,1)} %param.30), kind=kOutput, calls=%fused_computation.200 | convolution fusion | flops 4294967296 | bytes 12582912 | tf_op jit(solution)/shard_map/dot_general | solution.py:86
  208.0 92.1 %all-reduce.3.cloned.1.call-done = f32[8,4,32,1024]{3,2,1,0:T(8,128)} async-done(((f32[8,4,32,1024]{3,2,1,0:T(8,128)}), f32[8,4,32,1024]{3,2,1,0:T(8,128)}) %all-reduce.3.cloned.1.call-update) | async-done | bytes 4194320
  300.2 3.0 dynamic-slice_bitcast_fusion
  303.1 4.4 all-to-all-start
  307.9 15.6 %all-to-all-done = f32[32,8,1024]{2,0,1:T(8,128)S(1)} async-done(((f32[32,8,1024]{2,0,1:T(8,128)}), f32[32,8,1024]{2,0,1:T(8,128)S(1)}, u32[]{:S(2)}, u32[]{:S(2)}) %all-to-all-start) | async-done | bytes 1048608 | tf_op jit(solution)/shard_map/all_to_all | solution.py:97
  326.7 38.1 %all_gather.27 = bf16[512,64]{1,0:T(8,128)(2,1)S(1)} all-gather(bf16[16,64]{1,0:T(8,128)(2,1)S(1)} %convolution_convert_fusion.2), channel_id=1, replica_groups=mesh['dp'=4,'seq'=8,'expert'=4] {'seq','expert'}, dimensions={0}, use_global_device_ids=true | all-gather | bytes 67584 | tf_op jit(solution)/shard_map/all_gather | solution.py:135
  364.9 12.8 %all-gather.9.cloned.1.call-done = bf16[512,8192]{1,0:T(8,128)(2,1)} async-done(((bf16[16,8192]{1,0:T(8,128)(2,1)}), bf16[512,8192]{1,0:T(8,128)(2,1)}) %all-gather.9.cloned.1.call-update) | async-done | bytes 8388624 | tf_op jit(solution)/shard_map/all_gather | solution.py:134
  377.7 8.0 %mul.821 = f32[512,64,128]{2,1,0:T(8,128)} broadcast(bf16[512,64]{1,0:T(8,128)(2,1)S(1)} %all_gather.27), dimensions={0,1} | broadcast | bytes 16842752 | tf_op jit(solution)/shard_map/mul | solution.py:140
  385.6 18.4 %fusion.89 = f32[512,384]{1,0:T(8,128)S(1)} fusion(bf16[8192,384]{1,0:T(8,128)(2,1)} %param.35, f32[64,8,64,128]{3,2,1,0:T(8,128)} %bitcast.286, bf16[512,8192]{1,0:T(8,128)(2,1)S(1)} %copy-done.1), kind=kOutput, calls=%fused_computation.199 | convolution fusion | flops 3233808384 | bytes 32243712 | tf_op jit(solution)/shard_map/dot_general | solution.py:146
  404.0 28.3 %convolution_convert_fusion = bf16[512,8192]{1,0:T(8,128)(2,1)} fusion(bf16[384,8192]{1,0:T(8,128)(2,1)} %param.37, bf16[8192,384]{1,0:T(8,128)(2,1)} %param.36, f32[512,384]{1,0:T(8,128)S(1)} %fusion.89, f32[64,8,64,128]{3,2,1,0:T(8,128)} %bitcast.287, bf16[512,8192]{1,0:T(8,128)(2,1)} %all-gather.9.cloned.1.call-done), kind=kOutput, calls=%fused_computation.137 | convolution fusion | flops 6460407808 | bytes 46923776 | tf_op jit(solution)/shard_map/dot_general | solution.py:150
  433.2 91.7 %reduce-scatter.5.cloned.1.call-done = bf16[16,8192]{1,0:T(8,128)(2,1)} async-done(((bf16[512,8192]{1,0:T(8,128)(2,1)}), bf16[16,8192]{1,0:T(8,128)(2,1)}) %reduce-scatter.5.cloned.1.call-update) | async-done | bytes 262160 | tf_op jit(solution)/shard_map/reduce_scatter | solution.py:149
  524.9 2.1 fusion.50
  (281 shorter events, 93.8 us)
Async XLA Ops:
  6.5 425.8 %copy-start = (bf16[8192,16]{0,1:T(8,128)(2,1)S(1)}, bf16[8192,16]{0,1:T(8,128)(2,1)}, u32[]{:S(2)}) copy-start(bf16[8192,16]{0,1:T(8,128)(2,1)} %param.33) | copy-start | bytes 786436
  6.5 27.9 %copy-start.7 = (bf16[16,128]{1,0:T(8,128)(2,1)S(1)}, bf16[16,128]{1,0:T(8,128)(2,1)}, u32[]{:S(2)}) copy-start(bf16[16,128]{1,0:T(8,128)(2,1)} %param.28) | copy-start | bytes 12292
  6.5 85.0 %copy-start.5 = (f32[2048]{0:T(1024)S(1)}, f32[2048]{0:T(1024)}, u32[]{:S(2)}) copy-start(f32[2048]{0:T(1024)} %param.29) | copy-start | bytes 24580
  6.5 52.3 %all-gather.13.cloned.1.call-start = ((), (), s32[]{:S(2)}) async-start(), calls=%async_computation.6 | async-start | bytes 1179648 | tf_op jit(solution)/shard_map/all_gather | solution.py:11
  32.1 0.6 copy-start.2
  32.1 130.7 %copy-start.4 = (bf16[128,2048]{1,0:T(8,128)(2,1)S(1)}, bf16[128,2048]{1,0:T(8,128)(2,1)}, u32[]{:S(2)}) copy-start(bf16[128,2048]{1,0:T(8,128)(2,1)} %param.23) | copy-start | bytes 1572868
  32.7 51.2 %all-gather.11.cloned.1.call-start = ((), (), s32[]{:S(2)}) async-start(), calls=%async_computation.5 | async-start | bytes 1179648 | tf_op jit(solution)/shard_map/all_gather | solution.py:11
  34.4 163.1 %all-gather.7.cloned.1.call-start = ((), (), s32[]{:S(2)}) async-start(), calls=%async_computation.2 | async-start | bytes 4718592 | tf_op jit(solution)/shard_map/all_gather | solution.py:87
  165.1 42.3 %copy-start.9 = (u32[128]{0:T(128)S(1)}, u32[128]{0:T(128)}, u32[]{:S(2)}) copy-start(u32[128]{0:T(128)} %constant.87) | copy-start | bytes 1540
  165.2 135.0 %all-reduce.3.cloned.1.call-start = ((), (), s32[]{:S(2)}) async-start(), calls=%async_computation.7 | async-start | bytes 8388608
  207.4 100.2 %copy-start.8 = (s32[32,2]{0,1:T(2,128)S(1)}, s32[32,2]{0,1:T(2,128)}, u32[]{:S(2)}) copy-start(s32[32,2]{0,1:T(2,128)} %param.34) | copy-start | bytes 772
  207.4 116.2 %copy-start.3 = (bf16[32,8192]{1,0:T(8,128)(2,1)S(1)}, bf16[32,8192]{1,0:T(8,128)(2,1)}, u32[]{:S(2)}) copy-start(bf16[32,8192]{1,0:T(8,128)(2,1)} %param.31) | copy-start | bytes 1572868
  207.4 116.5 %copy-start.6 = (f32[8192]{0:T(1024)S(1)}, f32[8192]{0:T(1024)}, u32[]{:S(2)}) copy-start(f32[8192]{0:T(1024)} %param.32) | copy-start | bytes 98308
  303.1 20.4 %all-to-all-start = ((f32[32,8,1024]{2,0,1:T(8,128)}), f32[32,8,1024]{2,0,1:T(8,128)S(1)}, u32[]{:S(2)}, u32[]{:S(2)}) async-start(f32[32,8,1024]{2,0,1:T(8,128)} %dynamic-slice_bitcast_fusion), calls=%async_computation | async-start | bytes 2097152 | tf_op jit(solution)/shard_map/all_to_all | solution.py:97
  307.5 70.1 %all-gather.9.cloned.1.call-start = ((), (), s32[]{:S(2)}) async-start(), calls=%async_computation.3 | async-start | bytes 8650752 | tf_op jit(solution)/shard_map/all_gather | solution.py:134
  326.6 198.3 %reduce-scatter.5.cloned.1.call-start = ((), (), s32[]{:S(2)}) async-start(), calls=%async_computation.4 | async-start | bytes 8650752 | tf_op jit(solution)/shard_map/reduce_scatter | solution.py:149
  377.7 8.0 %copy-start.1 = (bf16[512,8192]{1,0:T(8,128)(2,1)S(1)}, bf16[512,8192]{1,0:T(8,128)(2,1)}, u32[]{:S(2)}) copy-start(bf16[512,8192]{1,0:T(8,128)(2,1)} %all-gather.9.cloned.1.call-done) | copy-start | bytes 25165828
Sparse Core Ops, SparseCore 0:
  32.9 25.9 all-gather.12
  60.5 23.3 all-gather.10
  165.3 32.1 all-gather.6
  207.6 92.5 all-reduce.2
  326.7 50.9 all-gather.8
  432.5 92.3 reduce-scatter.4
where the time goes:
time: 535 us; the launch traced here: 534 us
  waiting for transfers between devices  294 us (55%)
  other arithmetic  96.1 us (18%)
  matrix products  60.5 us (11%)
  blocking collectives  38.1 us (7%)
  local copies, waits for them, and re-layouts  25.5 us (5%)
  between operations  13.7 us (3%)
    unnamed x7, waiting for transfers between devices  92.2 us
    reduce_scatter x1, waiting for transfers between devices, on_device(): lax.psum_scatter(jnp.dot(active, down_weight, preferred_element_type=jnp....  91.7 us
    reduce_sum x48, other arithmetic, scan_advance(): y_now = jnp.sum(c_now[:, None] * state, axis=0) + skip_gain * x_now  54.8 us
    all_gather x2, waiting for transfers between devices, entering(): pieces = jax.tree.map(lambda part: lax.all_gather(part, axis), value)  49.4 us
    all_gather x1, blocking collectives, on_device(): lax.all_gather(send_scale, ('seq', 'expert'), axis=0, tiled=True)  38.1 us
    all_gather x1, waiting for transfers between devices, on_device(): lax.all_gather(gated, 'seq', axis=0, tiled=True)  32.3 us
    dot_general x1, matrix products, on_device(): jnp.dot(active, down_weight, preferred_element_type=jnp.float32)  28.3 us
    add x16, other arithmetic, end_advance(): jnp.exp(-step_now[None, :] * decay_rate) * state  18.7 us
  transfers between devices with their start and end apart: 7, of which 7 were waited for; matrix products, arithmetic and copies ran while one was open for 1% of the time, Pallas kernels for 0%

commit v1 on v0

--- a/solution.py
+++ b/solution.py
@@ -84,7 +84,9 @@
     scanned = scan_outputs(state_in, step_size, x_float, decay_rate, b_rows, c_rows, skip_gain)
     gated = (scanned * jax.nn.silu(z_in.astype(jnp.float32))).astype(jnp.bfloat16)
     column_part = jnp.dot(
-        lax.all_gather(gated, "seq", axis=0, tiled=True),
+        jnp.concatenate(
+            lax.all_to_all(jnp.stack([gated] * lax.axis_size("seq")), "seq", 0, 0), axis=0
+        ),
         out_proj,
         preferred_element_type=jnp.float32,
     )

time: 535 us -> 551 us (1.030)
  blocking collectives: 38.1 us -> 90.8 us
  waiting for transfers between devices: 294 us -> 261 us
    all_to_all x0 -> x1, blocking collectives: none -> 52.7 us  [on_device(): lax.all_to_all(jnp.stack([gated] * lax.axis_size('seq')), 'seq', 0, 0)]
    all_gather x1 -> x0, waiting for transfers between devices: 32.3 us -> none  [on_device(): lax.all_gather(gated, 'seq', axis=0, tiled=True)]
    unnamed x7 -> x6, waiting for transfers between devices: 92.2 us -> 91.7 us
  transfers between devices with their start and end apart: 7 -> 6, of which waited for: 7 -> 6; matrix products, arithmetic and copies ran while one was open for 1% -> 1% of each run, Pallas kernels for 0% -> 0%
where the time goes in v1:
time: 551 us; the launch traced here: 549 us
  waiting for transfers between devices  261 us (47%)
  other arithmetic  95.3 us (17%)
  blocking collectives  90.8 us (16%)
  matrix products  56.6 us (10%)
  local copies, waits for them, and re-layouts  26 us (5%)
  between operations  13.4 us (2%)
    reduce_scatter x1, waiting for transfers between devices, on_device(): lax.psum_scatter(jnp.dot(active, down_weight, preferred_element_type=jnp....  91.7 us
    unnamed x6, waiting for transfers between devices  91.7 us
    reduce_sum x48, other arithmetic, scan_advance(): y_now = jnp.sum(c_now[:, None] * state, axis=0) + skip_gain * x_now  54.8 us
    all_to_all x1, blocking collectives, on_device(): lax.all_to_all(jnp.stack([gated] * lax.axis_size('seq')), 'seq', 0, 0)  52.7 us
    all_gather x2, waiting for transfers between devices, entering(): pieces = jax.tree.map(lambda part: lax.all_gather(part, axis), value)  49.4 us
    all_gather x1, blocking collectives, on_device(): lax.all_gather(send_scale, ('seq', 'expert'), axis=0, tiled=True)  38.1 us
    dot_general x1, matrix products, on_device(): jnp.dot(active, down_weight, preferred_element_type=jnp.float32)  28.3 us
    add x16, other arithmetic, end_advance(): jnp.exp(-step_now[None, :] * decay_rate) * state  18.7 us
  transfers between devices with their start and end apart: 6, of which 6 were waited for; matrix products, arithmetic and copies ran while one was open for 1% of the time, Pallas kernels for 0%

profile of v1, /device:TPU:0, one launch (start us, length us, event | category | flops | bytes accessed | tf_op | source)
XLA Modules:
  0.0 549.2 jit_solution(2201608740314228060)
XLA Ops:
  8.5 1.7 fusion.69
  10.2 21.8 %while.38 = (s32[]{:T(128)}, f32[16,2048]{1,0:T(8,128)S(1)}, f32[16,8,2048]{2,1,0:T(8,128)S(1)}, f32[16,2048]{1,0:T(8,128)}, f32[16,8,2048]{2,1,0:T(8,128)S(1)},...) while((s32[]{:T(128)}, f32[16,2048]{1,0:T(8,128)S(1)}, ...), condition=%wide.region_2.3_spmd.clone, body=%wide.region_1.2_spmd.clone.sunk | while | flops 1114122 | bytes 789271 | solution.py:38
  32.8 1.6 multiply_exponential_fusion
  34.6 24.2 %all-gather.10.cloned.1.call-done = f32[128,2048]{1,0:T(8,128)} async-done(((f32[16,2048]{1,0:T(8,128)}), f32[128,2048]{1,0:T(8,128)}) %all-gather.10.cloned.1.call-update) | async-done | bytes 1048592 | tf_op jit(solution)/shard_map/all_gather | solution.py:11
  58.8 25.1 %all-gather.8.cloned.1.call-done = f32[128,2048]{1,0:T(8,128)} async-done(((f32[16,2048]{1,0:T(8,128)}), f32[128,2048]{1,0:T(8,128)}) %all-gather.8.cloned.1.call-update) | async-done | bytes 1048592 | tf_op jit(solution)/shard_map/all_gather | solution.py:11
  84.0 7.6 %while.39 = (s32[]{:T(128)}, f32[16,2048]{1,0:T(8,128)S(1)}, s32[]{:T(128)}, f32[8,16,2048]{2,1,0:T(8,128)}, f32[8,16,2048]{2,1,0:T(8,128)}, /*index=5*/s32[]{:T(128)}, s32[]{:T(128)}) while((s32[]{:T(128)}, f32[16,2048]{1,0:T(8,128)S(1)}, s32[]{:T(128)}, f32[8,16,2048]{2,1,0:T(8,128)}, f32[8,16,2048]{2,1,0:T(8,128)}, ...), condition=%wide.region_4.5_spmd.clone, body=%wide.region_3.4_spmd.clone.sunk | while | flops 131076 | bytes 524397 | solution.py:20
  91.6 71.2 %while.37 = (s32[]{:T(128)}, f32[16,2048]{1,0:T(8,128)S(1)}, f32[16,8,2048]{2,1,0:T(8,128)}, f32[16,8,2048]{2,1,0:T(8,128)S(1)}, f32[16,2048]{1,0:T(8,128)}, /*i...) while((s32[]{:T(128)}, f32[16,2048]{1,0:T(8,128)S(1)}, ...), condition=%wide.region_14.15_spmd, body=%wide.region_5.14_spmd.sunk | while | flops 2408457 | bytes 2078409 | solution.py:53
  92.9 1.2 multiply_reduce_fusion.11
  101.8 1.2 multiply_reduce_fusion.11
  115.1 1.2 multiply_reduce_fusion.11
  119.6 1.2 multiply_reduce_fusion.11
  128.5 1.2 multiply_reduce_fusion.11
  132.9 1.2 multiply_reduce_fusion.11
  141.8 1.2 multiply_reduce_fusion.11
  146.3 1.2 multiply_reduce_fusion.11
  150.7 1.2 multiply_reduce_fusion.11
  155.2 1.2 multiply_reduce_fusion.11
  159.6 1.2 multiply_reduce_fusion.11
  162.8 1.5 fusion.68
  164.9 52.7 %all_to_all.10 = bf16[8,128,2048]{2,1,0:T(8,128)(2,1)S(1)} all-to-all(bf16[8,128,2048]{2,1,0:T(8,128)(2,1)S(1)} %stack.2), channel_id=1, replica_groups=mesh['dp'=4,'seq'=8,'expert'=4] {'seq'}, dimensions={0} | all-to-all | bytes 8388608 | tf_op jit(solution)/shard_map/all_to_all | solution.py:88
  217.6 6.0 %fusion.51 = f32[8,4,32,1024]{3,2,1,0:T(8,128)} fusion(bf16[8,4,32,2048]{3,2,1,0:T(8,128)(2,1)S(1)} %bitcast.295, bf16[2048,1024]{1,0:T(8,128)(2,1)S(1)} %copy-done.9), kind=kOutput, calls=%fused_computation.142 | convolution fusion | flops 4294967296 | bytes 12582912 | tf_op jit(solution)/shard_map/dot_general | solution.py:86
  224.2 91.6 %all-reduce.3.cloned.1.call-done = f32[8,4,32,1024]{3,2,1,0:T(8,128)} async-done(((f32[8,4,32,1024]{3,2,1,0:T(8,128)}), f32[8,4,32,1024]{3,2,1,0:T(8,128)}) %all-reduce.3.cloned.1.call-update) | async-done | bytes 4194320
  315.9 3.0 dynamic-slice_bitcast_fusion
  318.8 4.4 all-to-all-start.1
  323.6 15.6 %all-to-all-done.1 = f32[32,8,1024]{2,0,1:T(8,128)S(1)} async-done(((f32[32,8,1024]{2,0,1:T(8,128)}), f32[32,8,1024]{2,0,1:T(8,128)S(1)}, u32[]{:S(2)}, u32[]{:S(2)}) %all-to-all-start.1) | async-done | bytes 1048608 | tf_op jit(solution)/shard_map/all_to_all | solution.py:99
  342.4 38.1 %all_gather.23 = bf16[512,64]{1,0:T(8,128)(2,1)S(1)} all-gather(bf16[16,64]{1,0:T(8,128)(2,1)S(1)} %convolution_convert_fusion.2), channel_id=1, replica_groups=mesh['dp'=4,'seq'=8,'expert'=4] {'seq','expert'}, dimensions={0}, use_global_device_ids=true | all-gather | bytes 67584 | tf_op jit(solution)/shard_map/all_gather | solution.py:137
  380.6 12.8 %all-gather.6.cloned.1.call-done = bf16[512,8192]{1,0:T(8,128)(2,1)} async-done(((bf16[16,8192]{1,0:T(8,128)(2,1)}), bf16[512,8192]{1,0:T(8,128)(2,1)}) %all-gather.6.cloned.1.call-update) | async-done | bytes 8388624 | tf_op jit(solution)/shard_map/all_gather | solution.py:136
  393.4 8.0 %mul.821 = f32[512,64,128]{2,1,0:T(8,128)} broadcast(bf16[512,64]{1,0:T(8,128)(2,1)S(1)} %all_gather.23), dimensions={0,1} | broadcast | bytes 16842752 | tf_op jit(solution)/shard_map/mul | solution.py:142
  401.4 18.4 %fusion.91 = f32[512,384]{1,0:T(8,128)S(1)} fusion(bf16[8192,384]{1,0:T(8,128)(2,1)} %param.35, f32[64,8,64,128]{3,2,1,0:T(8,128)} %bitcast.290, bf16[512,8192]{1,0:T(8,128)(2,1)S(1)} %copy-done.1), kind=kOutput, calls=%fused_computation.201 | convolution fusion | flops 3233808384 | bytes 32243712 | tf_op jit(solution)/shard_map/dot_general | solution.py:148
  419.7 28.3 %convolution_convert_fusion = bf16[512,8192]{1,0:T(8,128)(2,1)} fusion(bf16[384,8192]{1,0:T(8,128)(2,1)} %param.37, bf16[8192,384]{1,0:T(8,128)(2,1)} %param.36, f32[512,384]{1,0:T(8,128)S(1)} %fusion.91, f32[64,8,64,128]{3,2,1,0:T(8,128)} %bitcast.291, bf16[512,8192]{1,0:T(8,128)(2,1)} %all-gather.6.cloned.1.call-done), kind=kOutput, calls=%fused_computation.137 | convolution fusion | flops 6460407808 | bytes 46923776 | tf_op jit(solution)/shard_map/dot_general | solution.py:152
  448.9 91.7 %reduce-scatter.5.cloned.1.call-done = bf16[16,8192]{1,0:T(8,128)(2,1)} async-done(((bf16[512,8192]{1,0:T(8,128)(2,1)}), bf16[16,8192]{1,0:T(8,128)(2,1)}) %reduce-scatter.5.cloned.1.call-update) | async-done | bytes 262160 | tf_op jit(solution)/shard_map/reduce_scatter | solution.py:151
  540.6 2.1 fusion.50
  (282 shorter events, 94.2 us)
Async XLA Ops:
  6.5 441.5 %copy-start = (bf16[8192,16]{0,1:T(8,128)(2,1)S(1)}, bf16[8192,16]{0,1:T(8,128)(2,1)}, u32[]{:S(2)}) copy-start(bf16[8192,16]{0,1:T(8,128)(2,1)} %param.33) | copy-start | bytes 786436
  6.5 27.9 %copy-start.7 = (bf16[16,128]{1,0:T(8,128)(2,1)S(1)}, bf16[16,128]{1,0:T(8,128)(2,1)}, u32[]{:S(2)}) copy-start(bf16[16,128]{1,0:T(8,128)(2,1)} %param.28) | copy-start | bytes 12292
  6.5 85.1 %copy-start.5 = (f32[2048]{0:T(1024)S(1)}, f32[2048]{0:T(1024)}, u32[]{:S(2)}) copy-start(f32[2048]{0:T(1024)} %param.29) | copy-start | bytes 24580
  6.5 52.3 %all-gather.10.cloned.1.call-start = ((), (), s32[]{:S(2)}) async-start(), calls=%async_computation.6 | async-start | bytes 1179648 | tf_op jit(solution)/shard_map/all_gather | solution.py:11
  32.1 0.6 copy-start.2
  32.7 51.2 %all-gather.8.cloned.1.call-start = ((), (), s32[]{:S(2)}) async-start(), calls=%async_computation.5 | async-start | bytes 1179648 | tf_op jit(solution)/shard_map/all_gather | solution.py:11
  34.4 281.5 %all-reduce.3.cloned.1.call-start = ((), (), s32[]{:S(2)}) async-start(), calls=%async_computation.7 | async-start | bytes 8388608
  91.6 71.2 %copy-start.4 = (bf16[128,2048]{1,0:T(8,128)(2,1)S(1)}, bf16[128,2048]{1,0:T(8,128)(2,1)}, u32[]{:S(2)}) copy-start(bf16[128,2048]{1,0:T(8,128)(2,1)} %param.23) | copy-start | bytes 1572868
  164.3 53.2 %copy-start.9 = (bf16[2048,1024]{1,0:T(8,128)(2,1)S(1)}, bf16[2048,1024]{1,0:T(8,128)(2,1)}, u32[]{:S(2)}) copy-start(bf16[2048,1024]{1,0:T(8,128)(2,1)} %param.30) | copy-start | bytes 12582916
  217.6 6.1 %copy-start.10 = (u32[128]{0:T(128)S(1)}, u32[128]{0:T(128)}, u32[]{:S(2)}) copy-start(u32[128]{0:T(128)} %constant.87) | copy-start | bytes 1540
  223.6 99.7 %copy-start.8 = (s32[32,2]{0,1:T(2,128)S(1)}, s32[32,2]{0,1:T(2,128)}, u32[]{:S(2)}) copy-start(s32[32,2]{0,1:T(2,128)} %param.34) | copy-start | bytes 772
  223.6 115.7 %copy-start.3 = (bf16[32,8192]{1,0:T(8,128)(2,1)S(1)}, bf16[32,8192]{1,0:T(8,128)(2,1)}, u32[]{:S(2)}) copy-start(bf16[32,8192]{1,0:T(8,128)(2,1)} %param.31) | copy-start | bytes 1572868
  223.6 116.0 %copy-start.6 = (f32[8192]{0:T(1024)S(1)}, f32[8192]{0:T(1024)}, u32[]{:S(2)}) copy-start(f32[8192]{0:T(1024)} %param.32) | copy-start | bytes 98308
  318.8 20.4 %all-to-all-start.1 = ((f32[32,8,1024]{2,0,1:T(8,128)}), f32[32,8,1024]{2,0,1:T(8,128)S(1)}, u32[]{:S(2)}, u32[]{:S(2)}) async-start(f32[32,8,1024]{2,0,1:T(8,128)} %dynamic-slice_bitcast_fusion), calls=%async_computation.1 | async-start | bytes 2097152 | tf_op jit(solution)/shard_map/all_to_all | solution.py:99
  323.2 70.1 %all-gather.6.cloned.1.call-start = ((), (), s32[]{:S(2)}) async-start(), calls=%async_computation.3 | async-start | bytes 8650752 | tf_op jit(solution)/shard_map/all_gather | solution.py:136
  342.3 198.4 %reduce-scatter.5.cloned.1.call-start = ((), (), s32[]{:S(2)}) async-start(), calls=%async_computation.4 | async-start | bytes 8650752 | tf_op jit(solution)/shard_map/reduce_scatter | solution.py:151
  393.4 8.0 %copy-start.1 = (bf16[512,8192]{1,0:T(8,128)(2,1)S(1)}, bf16[512,8192]{1,0:T(8,128)(2,1)}, u32[]{:S(2)}) copy-start(bf16[512,8192]{1,0:T(8,128)(2,1)} %all-gather.6.cloned.1.call-done) | copy-start | bytes 25165828
Sparse Core Ops, SparseCore 0:
  32.9 25.9 all-gather.9
  60.5 23.3 all-gather.7
  223.8 92.0 all-reduce.2
  342.4 50.9 all-gather.5
  448.2 92.3 reduce-scatter.4
